TPU v7x, 32 devices: a whole 2x2x4 slice. The times are simulated.
32 devices in a mesh: mem: 8 (over z, x), tp: 4 (over y, core).
Axes of the slice: x: 2, y: 2, z: 4, core: 2. Of those that a mesh axis runs over, the one named last changes fastest.
Arguments:
- tokens: bfloat16 [3072, 2560], P(('mem', 'tp')), may hold values from -48 to 48
- input_weight: bfloat16 [2560, 6144], P(None, 'tp'), may hold values from -0.125 to 0.125
- output_weight: bfloat16 [2048, 2560], P('tp'), may hold values from -0.125 to 0.125
- gate_logit: float32 [16], P('tp'), may hold values from -2 to 2
- memory: bfloat16 [2, 32768, 2048], P(None, 'mem', 'tp'), may hold values from -48 to 48
- retrieved: int32 [24, 16], P('mem'), may hold values from 0 to 255, as said below
- block_home: int32 [256], replicated, may hold values from 0 to 255, as said below
Outputs:
- mixed: bfloat16 [3072, 2560], P(('mem', 'tp'))
Inputs may be any that keep to these rules, and one draw needn't show every extreme that they name: `block_home`: A permutation: each logical block names one stored block; stored block s lies with index s // 32 of mem, as its block s % 32. `retrieved`: each row names 16 different logical blocks; rows i * 3 to i * 3 + 2 are the query blocks of index i of mem. A row names at most 2 blocks held by one index of mem, and all rows of one index of mem together name at most 2 different blocks held by one index of mem.
All inputs are finite; a program needn't handle non-finite values.
Results may differ from a plain program's by a relative error of at most 0.023.
Values may be sent and summed in bfloat16 or wider, within the bound.
No kernel may reach another device: no remote copies, remote signals or barrier semaphores. Data moves between devices by JAX's collectives and lax.ppermute only.
A program may use at most 128 MiB of HBM per device.

v0:
```python
import jax
import jax.numpy as jnp
from jax import lax
from jax.sharding import PartitionSpec as P

HD = 128
BLK = 128
TOPB = 16
CAP = 2
NEG_FILL = -1e30


def from_behind(value, axis, steps):
    count = lax.axis_size(axis)
    initial, last = (max(0, -steps), min(count, count - steps))
    return lax.ppermute(value, axis, [(source, source + steps) for source in range(initial, last)])


def softmax_rows(scores, allowed):
    row_peak = jnp.max(jnp.where(allowed, scores, NEG_FILL), axis=-1, keepdims=True)
    weights = jnp.where(allowed, jnp.exp(scores - row_peak), 0.0)
    return (weights / jnp.sum(weights, axis=-1, keepdims=True)).astype(jnp.bfloat16)


def local(tokens, input_weight, output_weight, gate_logit, memory, retrieved, block_home):
    holder_count = lax.axis_size("mem")
    share_rows = tokens.shape[0]
    local_rows = share_rows * lax.axis_size("tp")
    groups = output_weight.shape[0] // HD
    score_scale = HD ** (-0.5)
    projected = jnp.dot(
        lax.all_gather(tokens, "tp", axis=0, tiled=True),
        input_weight,
        preferred_element_type=jnp.float32,
    )
    projected = projected.astype(jnp.bfloat16).reshape(local_rows, groups, 3, HD)
    queries = projected[:, :, 0]
    key_rows = projected[:, :, 1]
    value_rows = projected[:, :, 2]
    last_rows = jnp.stack([key_rows[-BLK:], value_rows[-BLK:]]).reshape(2, BLK, groups * HD)
    before = from_behind(last_rows, "mem", 1).reshape(2, BLK, groups, HD)
    near_keys = jnp.concatenate([before[0], key_rows], axis=0)
    near_values = jnp.concatenate([before[1], value_rows], axis=0)
    near_scores = (
        jnp.einsum("qgd,kgd->gqk", queries, near_keys, preferred_element_type=jnp.float32)
        * score_scale
    )
    query_index = lax.broadcasted_iota(jnp.int32, (local_rows, local_rows + BLK), 0)
    key_index = lax.broadcasted_iota(jnp.int32, (local_rows, local_rows + BLK), 1)
    first_key = lax.axis_index("mem") * local_rows - BLK
    allowed = (
        (key_index > query_index) & (key_index <= query_index + BLK) & (key_index + first_key >= 0)
    )
    near_probs = softmax_rows(near_scores, allowed[None])
    near_out = jnp.einsum(
        "gqk,kgd->qgd", near_probs, near_values, preferred_element_type=jnp.float32
    )
    blocks_here = retrieved.shape[0]
    entries = blocks_here * TOPB
    local_blocks = memory.shape[1] // BLK
    flat_blocks = retrieved.reshape(entries)
    home_slot = jnp.take(block_home, flat_blocks)
    holder = home_slot // local_blocks
    local_block = home_slot % local_blocks
    local_store = memory.reshape(2, local_blocks, BLK, groups * HD)
    entry_order = jnp.arange(entries)
    earlier = entry_order[None, :] < entry_order[:, None]
    same_owner = holder[:, None] == holder[None, :]
    same_block = home_slot[:, None] == home_slot[None, :]
    first = jnp.sum(same_block & earlier, axis=1) == 0
    first_entry = jnp.argmax(same_block, axis=1)
    before_first = entry_order[None, :] < first_entry[:, None]
    slot_of = jnp.sum(same_owner & before_first & first[None, :], axis=1)
    wanted_ids = jnp.zeros((holder_count, CAP), jnp.int32).at[holder, slot_of].set(local_block)
    picked = jnp.take(
        local_store,
        lax.all_to_all(wanted_ids, "mem", split_axis=0, concat_axis=0, tiled=True).reshape(
            holder_count * CAP
        ),
        axis=1,
    )
    fetched = lax.all_to_all(picked, "mem", split_axis=1, concat_axis=1, tiled=True)
    pool = holder_count * CAP
    far_keys = fetched[0].reshape(pool * BLK, groups, HD)
    far_values = fetched[1].reshape(pool * BLK, groups, HD)
    row_of = entry_order // TOPB
    member = jnp.zeros((blocks_here, pool), jnp.bool_).at[row_of, holder * CAP + slot_of].set(True)
    far_allowed = jnp.repeat(member, BLK, axis=1)[:, None, None, :]
    block_queries = queries.reshape(blocks_here, BLK, groups, HD)
    far_scores = (
        jnp.einsum("bqgd,kgd->bgqk", block_queries, far_keys, preferred_element_type=jnp.float32)
        * score_scale
    )
    far_probs = softmax_rows(far_scores, far_allowed)
    far_out = jnp.einsum(
        "bgqk,kgd->bqgd", far_probs, far_values, preferred_element_type=jnp.float32
    )
    far_out = far_out.reshape(local_rows, groups, HD)
    mixing = jax.nn.sigmoid(gate_logit)[None, :, None]
    attended = (
        (mixing * far_out + (1.0 - mixing) * near_out)
        .astype(jnp.bfloat16)
        .reshape(local_rows, groups * HD)
    )
    return lax.psum_scatter(
        jnp.dot(attended, output_weight, preferred_element_type=jnp.float32).astype(jnp.bfloat16),
        "tp",
        scatter_dimension=0,
        tiled=True,
    )


def solution(mesh):
    placed = (
        P(("mem", "tp"), None),
        P(None, "tp"),
        P("tp", None),
        P("tp"),
        P(None, "mem", "tp"),
        P("mem", None),
        P(),
    )
    return jax.shard_map(
        local, mesh=mesh, in_specs=placed, out_specs=P(("mem", "tp"), None), check_vma=False
    )
```

profile of v0, /device:TPU:0, one launch (start us, length us, event | category | flops | bytes accessed | tf_op | source)
XLA Modules:
  0.0 221.5 jit_solution(2529680987774456837)
XLA Ops:
  6.5 0.9 reshape.393
  7.4 0.8 reshape.394
  8.2 1.5 gather_fusion
  9.7 0.7 compare_reduce_fusion
  10.4 0.2 convert_reduce_fusion.1
  10.6 0.2 convert_reduce_fusion
  10.9 2.8 %scatter_fusion = s32[8,2]{0,1:T(2,128)S(1)} fusion(s32[8,2]{0,1:T(2,128)S(1)} %broadcast.458, s32[48]{0:T(128)S(1)} %fusion.41, s32[48]{0:T(128)S(1)} %get-tuple-element.11), kind=kCustom, calls=%fused_computation.2 | custom fusion | bytes 960 | tf_op jit(solution)/shard_map/scatter | solution.py:74
  13.6 0.1 copy.53
  13.7 13.5 %all_to_all.14 = s32[8,1,2]{2,1,0:T(1,128)S(1)} all-to-all(s32[8,1,2]{2,1,0:T(1,128)S(1)} %copy.53), channel_id=1, replica_groups=mesh['mem'=8,'tp'=4] {'mem'}, dimensions={0} | all-to-all | bytes 128 | tf_op jit(solution)/shard_map/all_to_all | solution.py:77
  27.2 0.1 reshape.397
  27.3 0.5 broadcast.518
  27.8 0.7 reduce.24
  28.5 0.1 reshape.395
  28.6 6.2 %gather_fusion.1 = bf16[16,2,128,512]{3,2,1,0:T(8,128)(2,1)} fusion(bf16[2,32,128,512]{3,2,1,0:T(8,128)(2,1)} %bitcast.89, s32[1024]{0:T(1024)S(1)} %pad_clamp_fusion), kind=kCustom, calls=%fused_computation.1 | custom fusion | bytes 8388672 | tf_op jit(solution)/shard_map/jit(_take)/gather | solution.py:75
  34.7 4.6 %select_bitcast_fusion = bf16[2,16,128,512]{3,2,0,1:T(8,128)(2,1)} fusion(bf16[16,2,128,512]{3,2,1,0:T(8,128)(2,1)} %gather_fusion.1, pred[16]{0:T(512)(128)(4,1)S(1)} %compare_and_fusion.1), kind=kLoop, calls=%fused_computation.18 | loop fusion | flops 2097152 | bytes 8388624 | tf_op jit(solution)/shard_map/jit(_take)/select_n | solution.py:75
  39.4 4.5 %all-to-all-start.1 = ((bf16[2,16,128,512]{3,2,0,1:T(8,128)(2,1)}), bf16[2,16,128,512]{3,2,0,1:T(8,128)(2,1)}, u32[]{:S(2)}, u32[]{:S(2)}) async-start(bf16[2,16,128,512]{3,2,0,1:T(8,128)(2,1)} %select_bitcast_fusion), calls=%async_computation.1 | async-start | bytes 8388608 | tf_op jit(solution)/shard_map/all_to_all | solution.py:82
  43.9 0.0 all-gather.2.cloned.1.call-start
  44.0 0.7 all-gather.2.cloned.1.call-update
  44.7 0.0 reduce-scatter.2.cloned.1.call-start
  44.7 2.8 %scatter_fusion.1 = pred[3,16]{1,0:T(4,128)(4,1)S(1)} fusion(pred[3,16]{1,0:T(4,128)(4,1)S(1)} %broadcast_in_dim.88, s32[48]{0:T(128)S(1)} %get-tuple-element.9, pred[48]{0:T(512)(128)(4,1)S(1)} %broadcast.492), kind=kCustom, calls=%fused_computation.3 | custom fusion | bytes 528 | tf_op jit(solution)/shard_map/scatter | solution.py:87
  47.6 0.1 broadcast_bitcast_fusion
  47.7 0.9 fusion.26
  48.5 21.0 %all-gather.2.cloned.1.call-done = bf16[384,2560]{1,0:T(8,128)(2,1)} async-done(((bf16[96,2560]{1,0:T(8,128)(2,1)}), bf16[384,2560]{1,0:T(8,128)(2,1)}) %all-gather.2.cloned.1.call-update) | async-done | bytes 1966096 | tf_op jit(solution)/shard_map/all_gather | solution.py:32
  69.5 8.1 %convolution_convert_fusion.1 = bf16[384,1536]{1,0:T(8,128)(2,1)} fusion(bf16[384,2560]{1,0:T(8,128)(2,1)} %all-gather.2.cloned.1.call-done, bf16[2560,1536]{1,0:T(8,128)(2,1)} %param.8), kind=kOutput, calls=%fused_computation.23 | convolution fusion | flops 3020488704 | bytes 11010048 | tf_op jit(solution)/shard_map/dot_general | solution.py:31
  77.6 2.4 %copy.56 = bf16[384,1536]{0,1:T(8,128)(2,1)} copy(bf16[384,1536]{1,0:T(8,128)(2,1)} %convolution_convert_fusion.1) | data formatting | bytes 2359296 | tf_op jit(solution)/shard_map/convert_element_type | solution.py:36
  80.0 1.0 fusion.51
  81.0 0.7 pad_maximum_fusion
  81.8 4.1 %collective-permute-start = (bf16[2,128,512]{1,2,0:T(8,128)(2,1)}, bf16[2,128,512]{1,2,0:T(8,128)(2,1)}, u32[]{:S(2)}, u32[]{:S(2)}) collective-permute-start(bf16[2,128,512]{1,2,0:T(8,128)(2,1)} %pad_maximum_fusion), channel_id=1, source_target_pairs={{0,4},{4,8},{8,12},{12,16},{16,20},{20,24},{24,28},{1,5},{5,9},{9,... | collective-permute-start | bytes 786440 | tf_op jit(solution)/shard_map/ppermute | solution.py:16
  85.9 2.1 slice_bitcast_fusion
  88.0 0.9 copy.76
  88.9 0.2 copy.78
  89.2 2.2 %collective-permute-done = bf16[2,128,512]{1,2,0:T(8,128)(2,1)} collective-permute-done((bf16[2,128,512]{1,2,0:T(8,128)(2,1)}, bf16[2,128,512]{1,2,0:T(8,128)(2,1)}, u32[]{:S(2)}, u32[]{:S(2)}) %collective-permute-start) | collective-permute-done | bytes 262176 | tf_op jit(solution)/shard_map/ppermute | solution.py:16
  91.4 1.0 fusion.52
  92.4 0.1 copy.64
  92.5 1.7 fusion.30
  94.2 3.7 %fusion.53 = (f32[4,384]{1,0:T(4,128)}, f32[4,384,512]{2,1,0:T(8,128)}) fusion(f32[4,384,512]{2,1,0:T(8,128)S(1)} %fusion.30, pred[384,512]{1,0:T(8,128)(4,1)S(1)} %copy-done.3), kind=kOutput, calls=%fused_computation.114 | output fusion | flops 4719103 | bytes 6494208 | tf_op jit(solution)/shard_map/sub | solution.py:21
  97.9 38.0 %all-to-all-done.1 = bf16[2,16,128,512]{3,2,0,1:T(8,128)(2,1)} async-done(((bf16[2,16,128,512]{3,2,0,1:T(8,128)(2,1)}), bf16[2,16,128,512]{3,2,0,1:T(8,128)(2,1)}, u32[]{:S(2)}, u32[]{:S(2)}) %all-to-all-start.1) | async-done | bytes 4194336 | tf_op jit(solution)/shard_map/all_to_all | solution.py:82
  135.9 4.6 %fusion.50 = (bf16[1,16,128,512]{3,2,0,1:T(8,128)(2,1)}, bf16[1,16,128,512]{3,2,0,1:T(8,128)(2,1)}) fusion(bf16[2,16,128,512]{3,2,0,1:T(8,128)(2,1)} %all-to-all-done.1), kind=kLoop, calls=%fused_computation.111 | loop fusion | bytes 8388608 | tf_op jit(solution)/shard_map/slice | solution.py:85
  140.6 4.0 %reshape.432 = bf16[2048,4,128]{2,1,0:T(4,128)(2,1)} reshape(bf16[1,16,128,512]{3,2,0,1:T(8,128)(2,1)} %get-tuple-element.14) | data formatting | bytes 4194304 | tf_op jit(solution)/shard_map/reshape;squeeze | solution.py:84
  144.5 4.0 %reshape.431 = bf16[2048,4,128]{2,1,0:T(4,128)(2,1)} reshape(bf16[1,16,128,512]{3,2,0,1:T(8,128)(2,1)} %get-tuple-element.13) | data formatting | bytes 4194304 | tf_op jit(solution)/shard_map/reshape;squeeze | solution.py:85
  148.6 3.4 %fusion.14 = f32[4,2048,3,128]{3,1,2,0:T(8,128)S(1)} fusion(bf16[3,128,4,128]{3,1,0,2:T(8,128)(2,1)S(1)} %bitcast.91, bf16[2048,4,128,1]{2,1,0,3:T(4,128)(2,1)} %bitcast.85), kind=kOutput, calls=%fused_computation.25 | convolution fusion | flops 805306368 | bytes 15073280 | tf_op jit(solution)/shard_map/bqgd,kgd->bgqk/dot_general | solution.py:91
  152.0 6.9 %fusion.54 = (f32[3,4,128]{2,0,1:T(4,128)S(1)}, f32[3,4,128,2048]{2,3,0,1:T(8,128)}) fusion(f32[4,2048,3,128]{3,1,2,0:T(8,128)S(1)} %fusion.14, pred[3,2048]{1,0:T(4,128)(4,1)S(1)} %bitcast.100), kind=kOutput, calls=%fused_computation.115 | output fusion | flops 18876416 | bytes 25178112 | tf_op jit(solution)/shard_map/sub | solution.py:21
  158.9 7.9 %fusion.9 = f32[4,128,3,128]{1,3,2,0:T(8,128)} fusion(f32[3,4,128,2048]{2,3,0,1:T(8,128)} %get-tuple-element.25, f32[3,4,128]{2,0,1:T(4,128)S(1)} %get-tuple-element.24, bf16[2048,4,128,1]{2,1,0,3:T(4,128)(2,1)S(1)} %bitcast.90), kind=kOutput, calls=%fused_computation.16 | convolution fusion | flops 811597824 | bytes 15472640 | tf_op jit(solution)/shard_map/bgqk,kgd->bqgd/dot_general | solution.py:95
  166.8 1.4 copy.61
  168.2 2.7 %fusion.24 = bf16[384,4,128]{0,2,1:T(8,128)(2,1)S(1)} fusion(f32[4,384,512]{2,1,0:T(8,128)} %get-tuple-element.23, f32[4,384]{1,0:T(4,128)S(1)} %copy-done.5, f32[384,4,128]{0,2,1:T(8,128)S(1)} %copy.61, bf16[384,4,128]{0,2,1:T(8,128)(2,1)} %get-tuple-element.15, bf16[128,4,128]{0,2,1:T(8,128)(2,1)S(1)} %bitcast.98, f32[4]{0:T(128)S(1)} %get-tuple-element.7, ...), kind=kOutput, calls=%fused_computation.35 | convolution fusion | flops 204734464 | bytes 4855840 | tf_op jit(solution)/shard_map/gqk,kgd->qgd/dot_general | solution.py:55
  171.0 2.5 %convolution_convert_fusion = bf16[384,2560]{1,0:T(8,128)(2,1)} fusion(bf16[384,512]{0,1:T(8,128)(2,1)S(1)} %bitcast.97, bf16[512,2560]{1,0:T(8,128)(2,1)S(1)} %copy-done), kind=kOutput, calls=%fused_computation.17 | convolution fusion | flops 1007616000 | bytes 4980736 | tf_op jit(solution)/shard_map/dot_general | solution.py:106
  173.5 0.0 reduce-scatter.2.cloned.1.call-update
  173.5 41.1 %reduce-scatter.2.cloned.1.call-done = bf16[96,2560]{1,0:T(8,128)(2,1)} async-done(((bf16[384,2560]{1,0:T(8,128)(2,1)}), bf16[96,2560]{1,0:T(8,128)(2,1)}) %reduce-scatter.2.cloned.1.call-update) | async-done | bytes 491536 | tf_op jit(solution)/shard_map/reduce_scatter | solution.py:105
  (29 shorter events, 0.2 us)
Async XLA Ops:
  6.5 164.4 %copy-start = (bf16[512,2560]{1,0:T(8,128)(2,1)S(1)}, bf16[512,2560]{1,0:T(8,128)(2,1)}, u32[]{:S(2)}) copy-start(bf16[512,2560]{1,0:T(8,128)(2,1)} %param.9) | copy-start | bytes 7864324
  39.4 96.6 %all-to-all-start.1 = ((bf16[2,16,128,512]{3,2,0,1:T(8,128)(2,1)}), bf16[2,16,128,512]{3,2,0,1:T(8,128)(2,1)}, u32[]{:S(2)}, u32[]{:S(2)}) async-start(bf16[2,16,128,512]{3,2,0,1:T(8,128)(2,1)} %select_bitcast_fusion), calls=%async_computation.1 | async-start | bytes 8388608 | tf_op jit(solution)/shard_map/all_to_all | solution.py:82
  43.9 25.6 %all-gather.2.cloned.1.call-start = ((), (), s32[]{:S(2)}) async-start(), calls=%async_computation.3 | async-start | bytes 2457600 | tf_op jit(solution)/shard_map/all_gather | solution.py:32
  44.7 170.0 %reduce-scatter.2.cloned.1.call-start = ((), (), s32[]{:S(2)}) async-start(), calls=%async_computation.4 | async-start | bytes 2457600 | tf_op jit(solution)/shard_map/reduce_scatter | solution.py:105
  77.6 8.3 %copy-start.4 = (f32[4]{0:T(128)S(1)}, f32[4]{0:T(128)}, u32[]{:S(2)}) copy-start(f32[4]{0:T(128)} %param.10) | copy-start | bytes 52
  81.8 9.6 %collective-permute-start = (bf16[2,128,512]{1,2,0:T(8,128)(2,1)}, bf16[2,128,512]{1,2,0:T(8,128)(2,1)}, u32[]{:S(2)}, u32[]{:S(2)}) collective-permute-start(bf16[2,128,512]{1,2,0:T(8,128)(2,1)} %pad_maximum_fusion), channel_id=1, source_target_pairs={{0,4},{4,8},{8,12},{12,16},{16,20},{20,24},{24,28},{1,5},{5,9},{9,... | collective-permute-start | bytes 786440 | tf_op jit(solution)/shard_map/ppermute | solution.py:16
  92.5 1.7 copy-start.3
  144.5 4.0 %copy-start.2 = (bf16[384,4,1,128]{3,0,1,2:T(8,128)(2,1)S(1)}, bf16[384,4,1,128]{3,0,1,2:T(8,128)(2,1)}, u32[]{:S(2)}) copy-start(bf16[384,4,1,128]{3,0,1,2:T(8,128)(2,1)} %copy.76) | copy-start | bytes 1179652
  152.0 6.9 %copy-start.1 = (bf16[2048,4,128]{2,1,0:T(4,128)(2,1)S(1)}, bf16[2048,4,128]{2,1,0:T(4,128)(2,1)}, u32[]{:S(2)}) copy-start(bf16[2048,4,128]{2,1,0:T(4,128)(2,1)} %reshape.431) | copy-start | bytes 6291460
  158.9 9.3 %copy-start.5 = (f32[4,384]{1,0:T(4,128)S(1)}, f32[4,384]{1,0:T(4,128)}, u32[]{:S(2)}) copy-start(f32[4,384]{1,0:T(4,128)} %get-tuple-element.22) | copy-start | bytes 18436
Sparse Core Ops, SparseCore 0:
  46.3 23.1 all-gather.1
  173.6 40.9 reduce-scatter.1
where the time goes:
time: 222 us; the launch traced here: 221 us
  waiting for transfers between devices  103 us (46%)
  local copies, waits for them, and re-layouts  37.6 us (17%)
  matrix products  26.2 us (12%)
  other arithmetic  18.7 us (8%)
  between operations  13.6 us (6%)
  blocking collectives  13.5 us (6%)
  starting transfers between devices  8.71 us (4%)
    reduce_scatter x1, waiting for transfers between devices, local(): lax.psum_scatter(jnp.dot(attended, output_weight, preferred_element_type=...  41.1 us
    all_to_all x1, waiting for transfers between devices, local(): lax.all_to_all(picked, 'mem', split_axis=1, concat_axis=1, tiled=True)  38 us
    all_gather x1, waiting for transfers between devices, local(): lax.all_gather(tokens, 'tp', axis=0, tiled=True)  21 us
    all_to_all x1, blocking collectives, local(): lax.all_to_all(wanted_ids, 'mem', split_axis=0, concat_axis=0, tiled=True)  13.5 us
    sub x2, other arithmetic, softmax_rows(): weights = jnp.where(allowed, jnp.exp(scores - row_peak), 0.0)  10.6 us
    dot_general x1, matrix products, local(): jnp.dot(lax.all_gather(tokens, 'tp', axis=0, tiled=True), input_weight, p...  8.05 us
    dot_general x1, matrix products, local(): jnp.einsum('bgqk,kgd->bqgd', far_probs, far_values, preferred_element_typ...  7.92 us
    gather x1, local copies, waits for them, and re-layouts, local(): jnp.take(local_store, lax.all_to_all(wanted_ids, 'mem', split_axis=0, con...  6.17 us
  transfers between devices with their start and end apart: 4, of which 4 were waited for; matrix products, arithmetic and copies ran while one was open for 12% of the time, Pallas kernels for 0%

commit v1 on v0

--- a/solution.py
+++ b/solution.py
@@ -8,6 +8,19 @@
 TOPB = 16
 CAP = 2
 NEG_FILL = -1e30
+
+
+def _press_widths(local_x, in_dim, patch):
+    extra, known = (local_x.shape[:in_dim], local_x.shape[in_dim + 1 :])
+    return jnp.moveaxis(local_x.reshape(*extra, patch, -1, *known), in_dim, 0)
+
+
+def _recast_pieces_all(z, pos_dim):
+    z = jnp.moveaxis(z, 0, pos_dim)
+    right_arr = z.shape
+    return z.reshape(
+        *right_arr[:pos_dim], right_arr[pos_dim] * right_arr[pos_dim + 1], *right_arr[pos_dim + 2 :]
+    )
 
 
 def from_behind(value, axis, steps):
@@ -72,11 +85,20 @@
     before_first = entry_order[None, :] < first_entry[:, None]
     slot_of = jnp.sum(same_owner & before_first & first[None, :], axis=1)
     wanted_ids = jnp.zeros((holder_count, CAP), jnp.int32).at[holder, slot_of].set(local_block)
+
+    def clear_strings_over_axis(x_in, axis_key, values, arr_in):
+        outer, vec_out = (lax.axis_size(axis_key), lax.axis_index(axis_key))
+        low = _press_widths(x_in, values, outer)
+        inbox = [low[vec_out]]
+        for k0 in range(1, outer):
+            main = low[vec_out ^ k0]
+            inbox.append(lax.ppermute(main, axis_key, [(k, k ^ k0) for k in range(outer)]))
+        low = jnp.stack(inbox, axis=0)[vec_out ^ jnp.arange(outer)]
+        return _recast_pieces_all(low, arr_in)
+
     picked = jnp.take(
         local_store,
-        lax.all_to_all(wanted_ids, "mem", split_axis=0, concat_axis=0, tiled=True).reshape(
-            holder_count * CAP
-        ),
+        clear_strings_over_axis(wanted_ids, "mem", 0, 0).reshape(holder_count * CAP),
         axis=1,
     )
     fetched = lax.all_to_all(picked, "mem", split_axis=1, concat_axis=1, tiled=True)

time: 222 us -> 224 us (level)
  blocking collectives: 13.5 us -> 0 us
  starting transfers between devices: 8.71 us -> 21.2 us
  waiting for transfers between devices: 103 us -> 107 us
    all_to_all x1 -> x0, blocking collectives: 13.5 us -> none  [local(): lax.all_to_all(wanted_ids, 'mem', split_axis=0, concat_axis=0, tiled=True)]
    ppermute x0 -> x7, starting transfers between devices: none -> 12.5 us  [clear_strings_over_axis(): lax.ppermute(main, axis_key, [(k, k ^ k0) for k in range(outer)])]
    ppermute x0 -> x7, waiting for transfers between devices: none -> 4.76 us  [clear_strings_over_axis(): lax.ppermute(main, axis_key, [(k, k ^ k0) for k in range(outer)])]
    gather x1 -> x2, local copies, waits for them, and re-layouts: 6.17 us -> 6.72 us  [the longest x1 6.17 us: local(): jnp.take(local_store, clear_strings_over_axis(wanted_ids, 'mem', 0, 0).re...]
    select_n x2 -> x3, other arithmetic: 4.63 us -> 4.63 us  [the longest x2 4.62 us: local(): jnp.take(local_store, clear_strings_over_axis(wanted_ids, 'mem', 0, 0).re...]
  transfers between devices with their start and end apart: 4 -> 11, of which waited for: 4 -> 6; matrix products, arithmetic and copies ran while one was open for 12% -> 12% of each run, Pallas kernels for 0% -> 0%
where the time goes in v1:
time: 224 us
  waiting for transfers between devices  107 us (48%)
  local copies, waits for them, and re-layouts  37.9 us (17%)
  matrix products  26.2 us (12%)
  starting transfers between devices  21.2 us (9%)
  other arithmetic  18.1 us (8%)
  between operations  13.7 us (6%)
    reduce_scatter x1, waiting for transfers between devices, local(): lax.psum_scatter(jnp.dot(attended, output_weight, preferred_element_type=...  41.1 us
    all_to_all x1, waiting for transfers between devices, local(): lax.all_to_all(picked, 'mem', split_axis=1, concat_axis=1, tiled=True)  36.9 us
    all_gather x1, waiting for transfers between devices, local(): lax.all_gather(tokens, 'tp', axis=0, tiled=True)  21 us
    ppermute x7, starting transfers between devices, clear_strings_over_axis(): lax.ppermute(main, axis_key, [(k, k ^ k0) for k in range(outer)])  12.5 us
    sub x2, other arithmetic, softmax_rows(): weights = jnp.where(allowed, jnp.exp(scores - row_peak), 0.0)  10.6 us
    dot_general x1, matrix products, local(): jnp.dot(lax.all_gather(tokens, 'tp', axis=0, tiled=True), input_weight, p...  8.05 us
    dot_general x1, matrix products, local(): jnp.einsum('bgqk,kgd->bqgd', far_probs, far_values, preferred_element_typ...  7.92 us
    gather x1, local copies, waits for them, and re-layouts, local(): jnp.take(local_store, clear_strings_over_axis(wanted_ids, 'mem', 0, 0).re...  6.17 us
  transfers between devices with their start and end apart: 11, of which 6 were waited for; matrix products, arithmetic and copies ran while one was open for 12% of the time, Pallas kernels for 0%

profile of v1, /device:TPU:0, one launch (start us, length us, event | category | flops | bytes accessed | tf_op | source)
XLA Modules:
  0.0 223.8 jit_solution(6233978918659090933)
XLA Ops:
  6.5 0.9 reshape.416
  7.4 0.8 reshape.417
  8.2 1.5 gather_fusion
  9.7 0.7 compare_reduce_fusion
  10.4 0.2 convert_reduce_fusion.1
  10.7 0.2 convert_reduce_fusion
  10.9 2.8 %scatter_fusion = s32[8,2]{0,1:T(2,128)S(1)} fusion(s32[8,2]{0,1:T(2,128)S(1)} %broadcast.489, s32[48]{0:T(128)S(1)} %fusion.43, s32[48]{0:T(128)S(1)} %get-tuple-element.11), kind=kCustom, calls=%fused_computation.3 | custom fusion | bytes 960 | tf_op jit(solution)/shard_map/scatter | solution.py:87
  13.8 5.1 %collective-permute-start.5 = (s32[1,2]{0,1:T(2,128)S(1)}, s32[1,2]{0,1:T(2,128)S(1)}, u32[]{:S(2)}, u32[]{:S(2)}) collective-permute-start(s32[1,2]{0,1:T(2,128)S(1)} %get-tuple-element.23), channel_id=1, source_target_pairs={{0,24},{4,28},{8,16},{12,20},{16,8},{20,12},{24,0},{28,4},{1,25},{... | collective-permute-start | bytes 32 | tf_op jit(solution)/shard_map/ppermute | solution.py:95
  18.8 1.1 collective-permute-start.6
  20.0 0.4 collective-permute-start
  20.4 3.1 %collective-permute-start.2 = (s32[1,2]{0,1:T(2,128)S(1)}, s32[1,2]{0,1:T(2,128)S(1)}, u32[]{:S(2)}, u32[]{:S(2)}) collective-permute-start(s32[1,2]{0,1:T(2,128)S(1)} %get-tuple-element.26), channel_id=1, source_target_pairs={{0,12},{4,8},{8,4},{12,0},{16,28},{20,24},{24,20},{28,16},{1,13},{... | collective-permute-start | bytes 32 | tf_op jit(solution)/shard_map/ppermute | solution.py:95
  23.5 2.2 collective-permute-start.3
  25.7 0.6 collective-permute-start.4
  26.3 1.7 collective-permute-done.3
  28.0 3.0 %collective-permute-done.4 = s32[1,2]{0,1:T(2,128)S(1)} collective-permute-done((s32[1,2]{0,1:T(2,128)S(1)}, s32[1,2]{0,1:T(2,128)S(1)}, u32[]{:S(2)}, u32[]{:S(2)}) %collective-permute-start.4) | collective-permute-done | bytes 40 | tf_op jit(solution)/shard_map/ppermute | solution.py:95
  31.1 0.1 stack.40
  31.3 0.6 gather_fusion.1
  32.0 6.2 %gather_fusion.2 = bf16[16,2,128,512]{3,2,1,0:T(8,128)(2,1)} fusion(bf16[2,32,128,512]{3,2,1,0:T(8,128)(2,1)} %bitcast.98, s32[1024]{0:T(1024)S(1)} %pad_clamp_fusion), kind=kCustom, calls=%fused_computation.2 | custom fusion | bytes 8388672 | tf_op jit(solution)/shard_map/jit(_take)/gather | solution.py:99
  38.2 4.6 %select_bitcast_fusion = bf16[2,16,128,512]{3,2,0,1:T(8,128)(2,1)} fusion(bf16[16,2,128,512]{3,2,1,0:T(8,128)(2,1)} %gather_fusion.2, pred[16]{0:T(512)(128)(4,1)S(1)} %compare_and_fusion.1), kind=kLoop, calls=%fused_computation.19 | loop fusion | flops 2097152 | bytes 8388624 | tf_op jit(solution)/shard_map/jit(_take)/select_n | solution.py:99
  42.8 4.5 %all-to-all-start = ((bf16[2,16,128,512]{3,2,0,1:T(8,128)(2,1)}), bf16[2,16,128,512]{3,2,0,1:T(8,128)(2,1)}, u32[]{:S(2)}, u32[]{:S(2)}) async-start(bf16[2,16,128,512]{3,2,0,1:T(8,128)(2,1)} %select_bitcast_fusion), calls=%async_computation | async-start | bytes 8388608 | tf_op jit(solution)/shard_map/all_to_all | solution.py:104
  47.4 0.7 all-gather.2.cloned.1.call-update
  48.2 2.8 %scatter_fusion.1 = pred[3,16]{1,0:T(4,128)(4,1)S(1)} fusion(pred[3,16]{1,0:T(4,128)(4,1)S(1)} %broadcast_in_dim.89, s32[48]{0:T(128)S(1)} %get-tuple-element.9, pred[48]{0:T(512)(128)(4,1)S(1)} %broadcast.527), kind=kCustom, calls=%fused_computation.4 | custom fusion | bytes 528 | tf_op jit(solution)/shard_map/scatter | solution.py:109
  51.1 0.9 fusion.26
  52.0 21.0 %all-gather.2.cloned.1.call-done = bf16[384,2560]{1,0:T(8,128)(2,1)} async-done(((bf16[96,2560]{1,0:T(8,128)(2,1)}), bf16[384,2560]{1,0:T(8,128)(2,1)}) %all-gather.2.cloned.1.call-update) | async-done | bytes 1966096 | tf_op jit(solution)/shard_map/all_gather | solution.py:45
  73.0 8.1 %convolution_convert_fusion.1 = bf16[384,1536]{1,0:T(8,128)(2,1)} fusion(bf16[384,2560]{1,0:T(8,128)(2,1)} %all-gather.2.cloned.1.call-done, bf16[2560,1536]{1,0:T(8,128)(2,1)} %param.8), kind=kOutput, calls=%fused_computation.24 | convolution fusion | flops 3020488704 | bytes 11010048 | tf_op jit(solution)/shard_map/dot_general | solution.py:44
  81.1 2.4 %copy.72 = bf16[384,1536]{0,1:T(8,128)(2,1)} copy(bf16[384,1536]{1,0:T(8,128)(2,1)} %convolution_convert_fusion.1) | data formatting | bytes 2359296 | tf_op jit(solution)/shard_map/convert_element_type | solution.py:49
  83.5 1.0 fusion.53
  84.5 0.7 pad_maximum_fusion
  85.2 4.1 %collective-permute-start.7 = (bf16[2,128,512]{1,2,0:T(8,128)(2,1)}, bf16[2,128,512]{1,2,0:T(8,128)(2,1)}, u32[]{:S(2)}, u32[]{:S(2)}) collective-permute-start(bf16[2,128,512]{1,2,0:T(8,128)(2,1)} %pad_maximum_fusion), channel_id=1, source_target_pairs={{0,4},{4,8},{8,12},{12,16},{16,20},{20,24},{24,28},{1,5},{5,9},{9,... | collective-permute-start | bytes 786440 | tf_op jit(solution)/shard_map/ppermute | solution.py:29
  89.3 2.1 slice_bitcast_fusion
  91.5 0.9 copy.92
  92.4 0.2 copy.94
  92.6 2.2 collective-permute-done.7
  94.8 1.0 fusion.54
  95.8 0.1 copy.80
  96.0 1.7 fusion.30
  97.7 3.7 %fusion.55 = (f32[4,384]{1,0:T(4,128)}, f32[4,384,512]{2,1,0:T(8,128)}) fusion(f32[4,384,512]{2,1,0:T(8,128)S(1)} %fusion.30, pred[384,512]{1,0:T(8,128)(4,1)S(1)} %copy-done.3), kind=kOutput, calls=%fused_computation.127 | output fusion | flops 4719103 | bytes 6494208 | tf_op jit(solution)/shard_map/sub | solution.py:34
  101.4 36.9 %all-to-all-done = bf16[2,16,128,512]{3,2,0,1:T(8,128)(2,1)} async-done(((bf16[2,16,128,512]{3,2,0,1:T(8,128)(2,1)}), bf16[2,16,128,512]{3,2,0,1:T(8,128)(2,1)}, u32[]{:S(2)}, u32[]{:S(2)}) %all-to-all-start) | async-done | bytes 4194336 | tf_op jit(solution)/shard_map/all_to_all | solution.py:104
  138.3 4.6 %fusion.52 = (bf16[1,16,128,512]{3,2,0,1:T(8,128)(2,1)}, bf16[1,16,128,512]{3,2,0,1:T(8,128)(2,1)}) fusion(bf16[2,16,128,512]{3,2,0,1:T(8,128)(2,1)} %all-to-all-done), kind=kLoop, calls=%fused_computation.124 | loop fusion | bytes 8388608 | tf_op jit(solution)/shard_map/slice | solution.py:107
  142.9 4.0 %reshape.465 = bf16[2048,4,128]{2,1,0:T(4,128)(2,1)} reshape(bf16[1,16,128,512]{3,2,0,1:T(8,128)(2,1)} %get-tuple-element.14) | data formatting | bytes 4194304 | tf_op jit(solution)/shard_map/reshape;squeeze | solution.py:106
  146.9 4.0 %reshape.464 = bf16[2048,4,128]{2,1,0:T(4,128)(2,1)} reshape(bf16[1,16,128,512]{3,2,0,1:T(8,128)(2,1)} %get-tuple-element.13) | data formatting | bytes 4194304 | tf_op jit(solution)/shard_map/reshape;squeeze | solution.py:107
  150.9 3.4 %fusion.14 = f32[4,2048,3,128]{3,1,2,0:T(8,128)S(1)} fusion(bf16[3,128,4,128]{3,1,0,2:T(8,128)(2,1)S(1)} %bitcast.100, bf16[2048,4,128,1]{2,1,0,3:T(4,128)(2,1)} %bitcast.94), kind=kOutput, calls=%fused_computation.26 | convolution fusion | flops 805306368 | bytes 15073280 | tf_op jit(solution)/shard_map/bqgd,kgd->bgqk/dot_general | solution.py:113
  154.3 6.9 %fusion.56 = (f32[3,4,128]{2,0,1:T(4,128)S(1)}, f32[3,4,128,2048]{2,3,0,1:T(8,128)}) fusion(f32[4,2048,3,128]{3,1,2,0:T(8,128)S(1)} %fusion.14, pred[3,2048]{1,0:T(4,128)(4,1)S(1)} %bitcast.108), kind=kOutput, calls=%fused_computation.128 | output fusion | flops 18876416 | bytes 25178112 | tf_op jit(solution)/shard_map/sub | solution.py:34
  161.2 7.9 %fusion.9 = f32[4,128,3,128]{1,3,2,0:T(8,128)} fusion(f32[3,4,128,2048]{2,3,0,1:T(8,128)} %get-tuple-element.33, f32[3,4,128]{2,0,1:T(4,128)S(1)} %get-tuple-element.32, bf16[2048,4,128,1]{2,1,0,3:T(4,128)(2,1)S(1)} %bitcast.99), kind=kOutput, calls=%fused_computation.17 | convolution fusion | flops 811597824 | bytes 15472640 | tf_op jit(solution)/shard_map/bgqk,kgd->bqgd/dot_general | solution.py:117
  169.1 1.4 copy.77
  170.5 2.7 %fusion.24 = bf16[384,4,128]{0,2,1:T(8,128)(2,1)S(1)} fusion(f32[4,384,512]{2,1,0:T(8,128)} %get-tuple-element.31, f32[4,384]{1,0:T(4,128)S(1)} %copy-done.5, f32[384,4,128]{0,2,1:T(8,128)S(1)} %copy.77, bf16[384,4,128]{0,2,1:T(8,128)(2,1)} %get-tuple-element.15, bf16[128,4,128]{0,2,1:T(8,128)(2,1)S(1)} %bitcast.107, f32[4]{0:T(128)S(1)} %get-tuple-element.7, ...), kind=kOutput, calls=%fused_computation.36 | convolution fusion | flops 204734464 | bytes 4855840 | tf_op jit(solution)/shard_map/gqk,kgd->qgd/dot_general | solution.py:68
  173.3 2.5 %convolution_convert_fusion = bf16[384,2560]{1,0:T(8,128)(2,1)} fusion(bf16[384,512]{0,1:T(8,128)(2,1)S(1)} %bitcast.106, bf16[512,2560]{1,0:T(8,128)(2,1)S(1)} %copy-done), kind=kOutput, calls=%fused_computation.18 | convolution fusion | flops 1007616000 | bytes 4980736 | tf_op jit(solution)/shard_map/dot_general | solution.py:128
  175.8 41.1 %reduce-scatter.2.cloned.1.call-done = bf16[96,2560]{1,0:T(8,128)(2,1)} async-done(((bf16[384,2560]{1,0:T(8,128)(2,1)}), bf16[96,2560]{1,0:T(8,128)(2,1)}) %reduce-scatter.2.cloned.1.call-update) | async-done | bytes 491536 | tf_op jit(solution)/shard_map/reduce_scatter | solution.py:127
  (45 shorter events, 0.7 us)
Async XLA Ops:
  6.5 166.8 %copy-start = (bf16[512,2560]{1,0:T(8,128)(2,1)S(1)}, bf16[512,2560]{1,0:T(8,128)(2,1)}, u32[]{:S(2)}) copy-start(bf16[512,2560]{1,0:T(8,128)(2,1)} %param.9) | copy-start | bytes 7864324
  13.8 9.7 %collective-permute-start.5 = (s32[1,2]{0,1:T(2,128)S(1)}, s32[1,2]{0,1:T(2,128)S(1)}, u32[]{:S(2)}, u32[]{:S(2)}) collective-permute-start(s32[1,2]{0,1:T(2,128)S(1)} %get-tuple-element.23), channel_id=1, source_target_pairs={{0,24},{4,28},{8,16},{12,20},{16,8},{20,12},{24,0},{28,4},{1,25},{... | collective-permute-start | bytes 32 | tf_op jit(solution)/shard_map/ppermute | solution.py:95
  18.8 6.9 %collective-permute-start.6 = (s32[1,2]{0,1:T(2,128)S(1)}, s32[1,2]{0,1:T(2,128)S(1)}, u32[]{:S(2)}, u32[]{:S(2)}) collective-permute-start(s32[1,2]{0,1:T(2,128)S(1)} %get-tuple-element.22), channel_id=1, source_target_pairs={{0,28},{4,24},{8,20},{12,16},{16,12},{20,8},{24,4},{28,0},{1,29},{... | collective-permute-start | bytes 32 | tf_op jit(solution)/shard_map/ppermute | solution.py:95
  20.0 6.3 %collective-permute-start = (s32[1,2]{0,1:T(2,128)S(1)}, s32[1,2]{0,1:T(2,128)S(1)}, u32[]{:S(2)}, u32[]{:S(2)}) collective-permute-start(s32[1,2]{0,1:T(2,128)S(1)} %get-tuple-element.28), channel_id=1, source_target_pairs={{0,4},{4,0},{8,12},{12,8},{16,20},{20,16},{24,28},{28,24},{1,5},{5... | collective-permute-start | bytes 32 | tf_op jit(solution)/shard_map/ppermute | solution.py:95
  20.4 6.0 %collective-permute-start.1 = (s32[1,2]{0,1:T(2,128)S(1)}, s32[1,2]{0,1:T(2,128)S(1)}, u32[]{:S(2)}, u32[]{:S(2)}) collective-permute-start(s32[1,2]{0,1:T(2,128)S(1)} %get-tuple-element.27), channel_id=1, source_target_pairs={{0,8},{4,12},{8,0},{12,4},{16,24},{20,28},{24,16},{28,20},{1,9},{5... | collective-permute-start | bytes 32 | tf_op jit(solution)/shard_map/ppermute | solution.py:95
  20.4 6.0 %collective-permute-start.2 = (s32[1,2]{0,1:T(2,128)S(1)}, s32[1,2]{0,1:T(2,128)S(1)}, u32[]{:S(2)}, u32[]{:S(2)}) collective-permute-start(s32[1,2]{0,1:T(2,128)S(1)} %get-tuple-element.26), channel_id=1, source_target_pairs={{0,12},{4,8},{8,4},{12,0},{16,28},{20,24},{24,20},{28,16},{1,13},{... | collective-permute-start | bytes 32 | tf_op jit(solution)/shard_map/ppermute | solution.py:95
  23.5 4.5 %collective-permute-start.3 = (s32[1,2]{0,1:T(2,128)S(1)}, s32[1,2]{0,1:T(2,128)S(1)}, u32[]{:S(2)}, u32[]{:S(2)}) collective-permute-start(s32[1,2]{0,1:T(2,128)S(1)} %get-tuple-element.25), channel_id=1, source_target_pairs={{0,16},{4,20},{8,24},{12,28},{16,0},{20,4},{24,8},{28,12},{1,17},{... | collective-permute-start | bytes 32 | tf_op jit(solution)/shard_map/ppermute | solution.py:95
  25.7 5.4 %collective-permute-start.4 = (s32[1,2]{0,1:T(2,128)S(1)}, s32[1,2]{0,1:T(2,128)S(1)}, u32[]{:S(2)}, u32[]{:S(2)}) collective-permute-start(s32[1,2]{0,1:T(2,128)S(1)} %get-tuple-element.24), channel_id=1, source_target_pairs={{0,20},{4,16},{8,28},{12,24},{16,4},{20,0},{24,12},{28,8},{1,21},{... | collective-permute-start | bytes 32 | tf_op jit(solution)/shard_map/ppermute | solution.py:95
  42.8 95.5 %all-to-all-start = ((bf16[2,16,128,512]{3,2,0,1:T(8,128)(2,1)}), bf16[2,16,128,512]{3,2,0,1:T(8,128)(2,1)}, u32[]{:S(2)}, u32[]{:S(2)}) async-start(bf16[2,16,128,512]{3,2,0,1:T(8,128)(2,1)} %select_bitcast_fusion), calls=%async_computation | async-start | bytes 8388608 | tf_op jit(solution)/shard_map/all_to_all | solution.py:104
  47.4 25.6 %all-gather.2.cloned.1.call-start = ((), (), s32[]{:S(2)}) async-start(), calls=%async_computation.2 | async-start | bytes 2457600 | tf_op jit(solution)/shard_map/all_gather | solution.py:45
  48.1 168.8 %reduce-scatter.2.cloned.1.call-start = ((), (), s32[]{:S(2)}) async-start(), calls=%async_computation.3 | async-start | bytes 2457600 | tf_op jit(solution)/shard_map/reduce_scatter | solution.py:127
  81.0 8.3 %copy-start.4 = (f32[4]{0:T(128)S(1)}, f32[4]{0:T(128)}, u32[]{:S(2)}) copy-start(f32[4]{0:T(128)} %param.10) | copy-start | bytes 52
  85.2 9.6 %collective-permute-start.7 = (bf16[2,128,512]{1,2,0:T(8,128)(2,1)}, bf16[2,128,512]{1,2,0:T(8,128)(2,1)}, u32[]{:S(2)}, u32[]{:S(2)}) collective-permute-start(bf16[2,128,512]{1,2,0:T(8,128)(2,1)} %pad_maximum_fusion), channel_id=1, source_target_pairs={{0,4},{4,8},{8,12},{12,16},{16,20},{20,24},{24,28},{1,5},{5,9},{9,... | collective-permute-start | bytes 786440 | tf_op jit(solution)/shard_map/ppermute | solution.py:29
  96.0 1.7 copy-start.3
  146.9 4.0 %copy-start.2 = (bf16[384,4,1,128]{3,0,1,2:T(8,128)(2,1)S(1)}, bf16[384,4,1,128]{3,0,1,2:T(8,128)(2,1)}, u32[]{:S(2)}) copy-start(bf16[384,4,1,128]{3,0,1,2:T(8,128)(2,1)} %copy.92) | copy-start | bytes 1179652
  154.3 6.9 %copy-start.1 = (bf16[2048,4,128]{2,1,0:T(4,128)(2,1)S(1)}, bf16[2048,4,128]{2,1,0:T(4,128)(2,1)}, u32[]{:S(2)}) copy-start(bf16[2048,4,128]{2,1,0:T(4,128)(2,1)} %reshape.464) | copy-start | bytes 6291460
  161.2 9.3 %copy-start.5 = (f32[4,384]{1,0:T(4,128)S(1)}, f32[4,384]{1,0:T(4,128)}, u32[]{:S(2)}) copy-start(f32[4,384]{1,0:T(4,128)} %get-tuple-element.30) | copy-start | bytes 18436
Sparse Core Ops, SparseCore 0:
  49.8 23.1 all-gather.1
  175.9 40.9 reduce-scatter.1
